TPU v7x, 128 devices: a whole 4x4x4 slice. The times are simulated.
128 devices in a mesh: layer: 2 (over z_hi), row: 8 (over y, core), col: 8 (over z_lo, x).
Axes of the slice: x: 4, y: 4, z: 4 (z_hi: 2, z_lo: 2; z = z_hi * 2 + z_lo), core: 2. Of those that a mesh axis runs over, the one named last changes fastest.
Arguments:
- density: bfloat16 [6400, 6400], P('row', 'col'), may hold values from -2 to 2
- density_mask: int32 [64, 64], P('row', 'col'), may hold values 0 or 1
- square_mask: int32 [64, 64], P('row', 'col'), may hold values 0 or 1
- result_mask: int32 [64, 64], P('row', 'col'), may hold values 0 or 1
- block_perm: int32 [64], replicated, may hold values from 0 to 63, as said below
Outputs:
- purified: bfloat16 [6400, 6400], P('row', 'col')
Inputs may be any that keep to these rules, and one draw needn't show every extreme that they name: `block_perm`: A permutation of the 64 block indices. For any two aligned groups of 8 indices, exactly 1 indices of the first group are mapped into the second group.
All inputs are finite; a program needn't handle non-finite values. No bound on the sum of `density_mask` or of `square_mask` or of `result_mask` on one device may be relied on, other than what follows from the above.
Results may differ from a plain program's by a relative error of at most 0.0049.
Values may be sent and summed in bfloat16 or wider, within the bound.
No kernel may reach another device: no remote copies, remote signals or barrier semaphores. Data moves between devices by JAX's collectives and lax.ppermute only.
A program may use at most 64 MiB of HBM per device.

v0:
```python
import jax
import jax.numpy as jnp
from jax import lax
from jax.sharding import PartitionSpec as P


def passed_along(array, axis, by):
    count = lax.axis_size(axis)
    return lax.ppermute(array, axis, [(i, (i + by) % count) for i in range(count)])


def apply_pattern(values, pattern):
    count = pattern.shape[0]
    width = values.shape[0] // count
    shaped = values.reshape(count, width, count, width)
    shaped = shaped * pattern[:, None, :, None].astype(values.dtype)
    return shaped.reshape(count * width, count * width)


def pieces_out(values, mapping, row_group, col_group, groups):
    tile_blocks = mapping.shape[0] // groups
    width = values.shape[0] // tile_blocks
    per_pair = tile_blocks // groups
    row_order = jnp.argsort(lax.dynamic_slice_in_dim(mapping, row_group * tile_blocks, tile_blocks))
    col_order = jnp.argsort(lax.dynamic_slice_in_dim(mapping, col_group * tile_blocks, tile_blocks))
    shaped = values.reshape(tile_blocks, width, tile_blocks, width)
    shaped = jnp.take(shaped, row_order, axis=0)
    shaped = jnp.take(shaped, col_order, axis=2)
    shaped = shaped.reshape(groups, per_pair, width, groups, per_pair, width)
    shaped = shaped.transpose(0, 3, 1, 2, 4, 5)
    return shaped.reshape(groups * groups, per_pair * width, per_pair * width)


def source_rows(mapping, group, tile_blocks, per_pair):
    source = lax.dynamic_slice_in_dim(mapping, group * tile_blocks, tile_blocks) // tile_blocks
    positions = jnp.arange(tile_blocks, dtype=jnp.int32)
    same_group = source[:, None] == source[None, :]
    earlier = positions[None, :] < positions[:, None]
    ranking = jnp.sum(jnp.logical_and(same_group, earlier).astype(jnp.int32), axis=1)
    return source * per_pair + ranking


def assemble(received, mapping, row_group, col_group, groups):
    tile_blocks = mapping.shape[0] // groups
    per_pair = tile_blocks // groups
    width = received.shape[1] // per_pair
    shaped = received.reshape(groups, groups, per_pair, width, per_pair, width)
    shaped = shaped.transpose(0, 2, 3, 1, 4, 5).reshape(tile_blocks, width, tile_blocks, width)
    shaped = jnp.take(shaped, source_rows(mapping, row_group, tile_blocks, per_pair), axis=0)
    shaped = jnp.take(shaped, source_rows(mapping, col_group, tile_blocks, per_pair), axis=2)
    return shaped.reshape(tile_blocks * width, tile_blocks * width)


def skew_cols(values, amount, groups):
    for bit_index in range(groups.bit_length() - 1):
        moved = passed_along(values, "col", -(1 << bit_index))
        values = jnp.where(amount // (1 << bit_index) % 2 == 1, moved, values)
    return values


def skew_square(values, amount, groups):
    for bit_index in range(groups.bit_length() - 1):
        moved = passed_along(values, "col", -(1 << bit_index))
        values = jnp.where(amount // (1 << bit_index) % 2 == 1, moved, values)
    return values


def skew_rows(values, amount, groups):
    for bit_index in range(groups.bit_length() - 1):
        moved = passed_along(values, "row", -(1 << bit_index))
        values = jnp.where(amount // (1 << bit_index) % 2 == 1, moved, values)
    return values


def square_pass(left, right, steps):
    total = jnp.zeros((left.shape[0], right.shape[1]), jnp.float32)
    stored = []
    for step_index in range(steps):
        stored.append(right)
        total = total + jnp.dot(left, right, preferred_element_type=jnp.float32)
        if step_index + 1 < steps:
            left = passed_along(left, "col", -1)
            right = passed_along(right, "row", -1)
    return (total, stored)


def cube_pass(left, right, steps):
    total = jnp.zeros((left.shape[0], right.shape[1]), jnp.float32)
    for step_index in range(steps):
        factor = right
        total = total + jnp.dot(left, factor, preferred_element_type=jnp.float32)
        if step_index + 1 < steps:
            left = passed_along(left, "col", -1)
            right = passed_along(right, "row", -1)
    return total


def per_device(density, density_mask, square_mask, result_mask, block_perm):
    groups = lax.axis_size("row")
    steps = groups // lax.axis_size("layer")
    row_id = lax.axis_index("row")
    col_id = lax.axis_index("col")
    offset = lax.axis_index("layer") * steps
    inverse = jnp.argsort(block_perm)
    masked = apply_pattern(density, density_mask)
    pieces = pieces_out(masked, block_perm, row_id, col_id, groups)
    received = lax.all_to_all(pieces, ("row", "col"), split_axis=0, concat_axis=0, tiled=True)
    grid_tile = assemble(received, inverse, row_id, col_id, groups)
    left = skew_cols(grid_tile, (row_id + offset) % groups, groups)
    right = skew_rows(grid_tile, (col_id + offset) % groups, groups)
    square_part, stored = square_pass(left, right, steps)
    square_full = lax.psum(square_part, "layer")
    square = apply_pattern(square_full, square_mask).astype(jnp.bfloat16)
    square_left = skew_square(square, (row_id + offset) % groups, groups)
    cube_part = cube_pass(square_left, right, steps)
    cube = lax.psum(cube_part, "layer")
    result = apply_pattern(3.0 * square.astype(jnp.float32) - 2.0 * cube, result_mask).astype(
        jnp.bfloat16
    )
    outgoing = pieces_out(result, inverse, row_id, col_id, groups)
    returned = lax.all_to_all(outgoing, ("row", "col"), split_axis=0, concat_axis=0, tiled=True)
    return assemble(returned, block_perm, row_id, col_id, groups)


def solution(mesh):
    in_specs = (P("row", "col"), P("row", "col"), P("row", "col"), P("row", "col"), P())
    out_specs = P("row", "col")
    return jax.shard_map(
        per_device, mesh=mesh, in_specs=in_specs, out_specs=out_specs, check_vma=False
    )
```

profile of v0, /device:TPU:0, one launch (start us, length us, event | category | flops | bytes accessed | tf_op | source)
XLA Modules:
  0.0 729.8 jit_solution(15575496370506805132)
XLA Ops:
  12.0 3.4 reshape.66
  22.6 9.4 %all-to-all-start = ((bf16[64,100,100]{2,1,0:T(8,128)(2,1)}), bf16[64,100,100]{2,1,0:T(8,128)(2,1)S(1)}, u32[]{:S(2)}, u32[]{:S(2)}) async-start(bf16[64,100,100]{2,1,0:T(8,128)(2,1)} %copy.37), calls=%async_computation | async-start | bytes 3407872 | tf_op jit(solution)/shard_map/all_to_all | solution.py:107
  32.4 24.3 %all-to-all-done = bf16[64,100,100]{2,1,0:T(8,128)(2,1)S(1)} async-done(((bf16[64,100,100]{2,1,0:T(8,128)(2,1)}), bf16[64,100,100]{2,1,0:T(8,128)(2,1)S(1)}, u32[]{:S(2)}, u32[]{:S(2)}) %all-to-all-start) | async-done | bytes 1280032 | tf_op jit(solution)/shard_map/all_to_all | solution.py:107
  62.5 14.1 %collective-permute-start = (bf16[800,800]{1,0:T(8,128)(2,1)S(1)}, bf16[800,800]{1,0:T(8,128)(2,1)S(1)}, u32[]{:S(2)}, u32[]{:S(2)}) collective-permute-start(bf16[800,800]{1,0:T(8,128)(2,1)S(1)} %reshape.71), channel_id=1, source_target_pairs={{0,7},{1,0},{2,1},{3,2},{4,3},{5,4},{6,5},{7,6},{8,15},{9,8},{10,9... | collective-permute-start | bytes 3840008 | tf_op jit(solution)/shard_map/ppermute | solution.py:9
  76.6 31.9 %collective-permute-done = bf16[800,800]{1,0:T(8,128)(2,1)S(1)} collective-permute-done((bf16[800,800]{1,0:T(8,128)(2,1)S(1)}, bf16[800,800]{1,0:T(8,128)(2,1)S(1)}, u32[]{:S(2)}, u32[]{:S(2)}) %collective-permute-start) | collective-permute-done | bytes 1280032 | tf_op jit(solution)/shard_map/ppermute | solution.py:9
  113.0 32.2 %collective-permute-done.4 = bf16[800,800]{1,0:T(8,128)(2,1)} collective-permute-done((bf16[800,800]{1,0:T(8,128)(2,1)S(1)}, bf16[800,800]{1,0:T(8,128)(2,1)}, u32[]{:S(2)}, u32[]{:S(2)}) %collective-permute-start.4) | collective-permute-done | bytes 1280032 | tf_op jit(solution)/shard_map/ppermute | solution.py:9
  149.1 31.2 %collective-permute-done.5 = bf16[800,800]{1,0:T(8,128)(2,1)} collective-permute-done((bf16[800,800]{1,0:T(8,128)(2,1)S(1)}, bf16[800,800]{1,0:T(8,128)(2,1)}, u32[]{:S(2)}, u32[]{:S(2)}) %collective-permute-start.5) | collective-permute-done | bytes 1280032 | tf_op jit(solution)/shard_map/ppermute | solution.py:9
  181.9 3.8 collective-permute-start.6
  185.7 11.2 %collective-permute-done.7 = bf16[800,800]{1,0:T(8,128)(2,1)S(1)} collective-permute-done((bf16[800,800]{1,0:T(8,128)(2,1)S(1)}, bf16[800,800]{1,0:T(8,128)(2,1)S(1)}, u32[]{:S(2)}, u32[]{:S(2)}) %collective-permute-start.7) | collective-permute-done | bytes 1280032 | tf_op jit(solution)/shard_map/ppermute | solution.py:9
  196.9 3.1 collective-permute-start.9
  200.0 15.5 %collective-permute-done.6 = bf16[800,800]{1,0:T(8,128)(2,1)S(1)} collective-permute-done((bf16[800,800]{1,0:T(8,128)(2,1)S(1)}, bf16[800,800]{1,0:T(8,128)(2,1)S(1)}, u32[]{:S(2)}, u32[]{:S(2)}) %collective-permute-start.6) | collective-permute-done | bytes 1280032 | tf_op jit(solution)/shard_map/ppermute | solution.py:9
  215.5 4.6 collective-permute-start.8
  222.2 26.8 %collective-permute-done.8 = bf16[800,800]{1,0:T(8,128)(2,1)S(1)} collective-permute-done((bf16[800,800]{1,0:T(8,128)(2,1)S(1)}, bf16[800,800]{1,0:T(8,128)(2,1)S(1)}, u32[]{:S(2)}, u32[]{:S(2)}) %collective-permute-start.8) | collective-permute-done | bytes 1280032 | tf_op jit(solution)/shard_map/ppermute | solution.py:9
  249.1 4.6 collective-permute-start.10
  259.1 22.7 %collective-permute-done.10 = bf16[800,800]{1,0:T(8,128)(2,1)S(1)} collective-permute-done((bf16[800,800]{1,0:T(8,128)(2,1)S(1)}, bf16[800,800]{1,0:T(8,128)(2,1)S(1)}, u32[]{:S(2)}, u32[]{:S(2)}) %collective-permute-start.10) | collective-permute-done | bytes 1280032 | tf_op jit(solution)/shard_map/ppermute | solution.py:9
  281.8 3.5 add_add_fusion.1
  288.4 91.6 %all-reduce.3.cloned.1.call-done = f32[800,800]{1,0:T(8,128)} async-done(((f32[800,800]{1,0:T(8,128)}), f32[800,800]{1,0:T(8,128)}) %all-reduce.3.cloned.1.call-update) | async-done | bytes 2560016 | tf_op jit(solution)/shard_map/psum | solution.py:112
  380.1 2.9 multiply_convert_fusion.1
  385.9 30.5 %collective-permute-done.12 = bf16[800,800]{1,0:T(8,128)(2,1)S(1)} collective-permute-done((bf16[800,800]{1,0:T(8,128)(2,1)S(1)}, bf16[800,800]{1,0:T(8,128)(2,1)S(1)}, u32[]{:S(2)}, u32[]{:S(2)}) %collective-permute-start.12) | collective-permute-done | bytes 1280032 | tf_op jit(solution)/shard_map/ppermute | solution.py:9
  419.4 30.9 %collective-permute-done.13 = bf16[800,800]{1,0:T(8,128)(2,1)S(1)} collective-permute-done((bf16[800,800]{1,0:T(8,128)(2,1)S(1)}, bf16[800,800]{1,0:T(8,128)(2,1)S(1)}, u32[]{:S(2)}, u32[]{:S(2)}) %collective-permute-start.13) | collective-permute-done | bytes 1280032 | tf_op jit(solution)/shard_map/ppermute | solution.py:9
  451.9 29.9 %collective-permute-done.14 = bf16[800,800]{1,0:T(8,128)(2,1)S(1)} collective-permute-done((bf16[800,800]{1,0:T(8,128)(2,1)S(1)}, bf16[800,800]{1,0:T(8,128)(2,1)S(1)}, u32[]{:S(2)}, u32[]{:S(2)}) %collective-permute-start.14) | collective-permute-done | bytes 1280032 | tf_op jit(solution)/shard_map/ppermute | solution.py:9
  482.1 5.6 collective-permute-start.15
  487.6 27.9 %collective-permute-done.15 = bf16[800,800]{1,0:T(8,128)(2,1)S(1)} collective-permute-done((bf16[800,800]{1,0:T(8,128)(2,1)S(1)}, bf16[800,800]{1,0:T(8,128)(2,1)S(1)}, u32[]{:S(2)}, u32[]{:S(2)}) %collective-permute-start.15) | collective-permute-done | bytes 1280032 | tf_op jit(solution)/shard_map/ppermute | solution.py:9
  515.6 4.6 collective-permute-start.16
  520.1 27.1 %collective-permute-done.16 = bf16[800,800]{1,0:T(8,128)(2,1)S(1)} collective-permute-done((bf16[800,800]{1,0:T(8,128)(2,1)S(1)}, bf16[800,800]{1,0:T(8,128)(2,1)S(1)}, u32[]{:S(2)}, u32[]{:S(2)}) %collective-permute-start.16) | collective-permute-done | bytes 1280032 | tf_op jit(solution)/shard_map/ppermute | solution.py:9
  547.2 4.6 collective-permute-start.17
  557.2 20.8 %collective-permute-done.17 = bf16[800,800]{1,0:T(8,128)(2,1)S(1)} collective-permute-done((bf16[800,800]{1,0:T(8,128)(2,1)S(1)}, bf16[800,800]{1,0:T(8,128)(2,1)S(1)}, u32[]{:S(2)}, u32[]{:S(2)}) %collective-permute-start.17) | collective-permute-done | bytes 1280032 | tf_op jit(solution)/shard_map/ppermute | solution.py:9
  578.0 3.5 add_add_fusion
  586.9 84.0 %all-reduce.5.cloned.1.call-done = f32[800,800]{1,0:T(8,128)} async-done(((f32[800,800]{1,0:T(8,128)}), f32[800,800]{1,0:T(8,128)}) %all-reduce.5.cloned.1.call-update) | async-done | bytes 2560016 | tf_op jit(solution)/shard_map/psum | solution.py:116
  670.9 3.6 multiply_convert_fusion
  683.4 7.8 %all-to-all-start.1 = ((bf16[64,100,100]{2,1,0:T(8,128)(2,1)}), bf16[64,100,100]{2,1,0:T(8,128)(2,1)S(1)}, u32[]{:S(2)}, u32[]{:S(2)}) async-start(bf16[64,100,100]{2,1,0:T(8,128)(2,1)} %copy.44), calls=%async_computation.1 | async-start | bytes 3407872 | tf_op jit(solution)/shard_map/all_to_all | solution.py:121
  691.6 24.4 %all-to-all-done.1 = bf16[64,100,100]{2,1,0:T(8,128)(2,1)S(1)} async-done(((bf16[64,100,100]{2,1,0:T(8,128)(2,1)}), bf16[64,100,100]{2,1,0:T(8,128)(2,1)S(1)}, u32[]{:S(2)}, u32[]{:S(2)}) %all-to-all-start.1) | async-done | bytes 1280032 | tf_op jit(solution)/shard_map/all_to_all | solution.py:121
  (133 shorter events, 73.4 us)
Async XLA Ops:
  6.5 8.9 %copy-start.6 = (s32[8,8]{1,0:T(8,128)S(1)}, s32[8,8]{1,0:T(8,128)}, u32[]{:S(2)}) copy-start(s32[8,8]{1,0:T(8,128)} %param.10) | copy-start | bytes 772
  22.6 34.2 %all-to-all-start = ((bf16[64,100,100]{2,1,0:T(8,128)(2,1)}), bf16[64,100,100]{2,1,0:T(8,128)(2,1)S(1)}, u32[]{:S(2)}, u32[]{:S(2)}) async-start(bf16[64,100,100]{2,1,0:T(8,128)(2,1)} %copy.37), calls=%async_computation | async-start | bytes 3407872 | tf_op jit(solution)/shard_map/all_to_all | solution.py:107
  32.0 348.1 %all-reduce.3.cloned.1.call-start = ((), (), s32[]{:S(2)}) async-start(), calls=%async_computation.2 | async-start | bytes 5734400 | tf_op jit(solution)/shard_map/psum | solution.py:112
  62.5 46.0 %collective-permute-start = (bf16[800,800]{1,0:T(8,128)(2,1)S(1)}, bf16[800,800]{1,0:T(8,128)(2,1)S(1)}, u32[]{:S(2)}, u32[]{:S(2)}) collective-permute-start(bf16[800,800]{1,0:T(8,128)(2,1)S(1)} %reshape.71), channel_id=1, source_target_pairs={{0,7},{1,0},{2,1},{3,2},{4,3},{5,4},{6,5},{7,6},{8,15},{9,8},{10,9... | collective-permute-start | bytes 3840008 | tf_op jit(solution)/shard_map/ppermute | solution.py:9
  76.6 33.0 %collective-permute-start.3 = (bf16[800,800]{1,0:T(8,128)(2,1)S(1)}, bf16[800,800]{1,0:T(8,128)(2,1)}, u32[]{:S(2)}, u32[]{:S(2)}) collective-permute-start(bf16[800,800]{1,0:T(8,128)(2,1)S(1)} %reshape.71), channel_id=1, source_target_pairs={{0,56},{8,0},{16,8},{24,16},{32,24},{40,32},{48,40},{56,48},{1,57}... | collective-permute-start | bytes 3840008 | tf_op jit(solution)/shard_map/ppermute | solution.py:9
  111.0 34.1 %collective-permute-start.4 = (bf16[800,800]{1,0:T(8,128)(2,1)S(1)}, bf16[800,800]{1,0:T(8,128)(2,1)}, u32[]{:S(2)}, u32[]{:S(2)}) collective-permute-start(bf16[800,800]{1,0:T(8,128)(2,1)S(1)} %get-tuple-element.33), channel_id=1, source_target_pairs={{0,48},{8,56},{16,0},{24,8},{32,16},{40,24},{48,32},{56,40},{1,49}... | collective-permute-start | bytes 3840008 | tf_op jit(solution)/shard_map/ppermute | solution.py:9
  112.1 35.3 %collective-permute-start.1 = (bf16[800,800]{1,0:T(8,128)(2,1)}, bf16[800,800]{1,0:T(8,128)(2,1)}, u32[]{:S(2)}, u32[]{:S(2)}) collective-permute-start(bf16[800,800]{1,0:T(8,128)(2,1)} %get-tuple-element.34), channel_id=1, source_target_pairs={{0,6},{1,7},{2,0},{3,1},{4,2},{5,3},{6,4},{7,5},{8,14},{9,15},{10,... | collective-permute-start | bytes 3840008 | tf_op jit(solution)/shard_map/ppermute | solution.py:9
  145.4 34.9 %collective-permute-start.5 = (bf16[800,800]{1,0:T(8,128)(2,1)S(1)}, bf16[800,800]{1,0:T(8,128)(2,1)}, u32[]{:S(2)}, u32[]{:S(2)}) collective-permute-start(bf16[800,800]{1,0:T(8,128)(2,1)S(1)} %broadcast_select_fusion.5), channel_id=1, source_target_pairs={{0,32},{8,40},{16,48},{24,56},{32,0},{40,8},{48,16},{56,24},{1,33}... | collective-permute-start | bytes 3840008 | tf_op jit(solution)/shard_map/ppermute | solution.py:9
  148.9 32.8 %collective-permute-start.2 = (bf16[800,800]{1,0:T(8,128)(2,1)S(1)}, bf16[800,800]{1,0:T(8,128)(2,1)}, u32[]{:S(2)}, u32[]{:S(2)}) collective-permute-start(bf16[800,800]{1,0:T(8,128)(2,1)S(1)} %broadcast_select_fusion.10), channel_id=1, source_target_pairs={{0,4},{1,5},{2,6},{3,7},{4,0},{5,1},{6,2},{7,3},{8,12},{9,13},{10,... | collective-permute-start | bytes 3840008 | tf_op jit(solution)/shard_map/ppermute | solution.py:9
  180.4 73.3 %copy-start.3 = (bf16[800,800]{1,0:T(8,128)(2,1)}, bf16[800,800]{1,0:T(8,128)(2,1)S(1)}, u32[]{:S(2)}) copy-start(bf16[800,800]{1,0:T(8,128)(2,1)S(1)} %broadcast_select_fusion.6) | copy-start | bytes 3840004
  180.4 16.5 %collective-permute-start.7 = (bf16[800,800]{1,0:T(8,128)(2,1)S(1)}, bf16[800,800]{1,0:T(8,128)(2,1)S(1)}, u32[]{:S(2)}, u32[]{:S(2)}) collective-permute-start(bf16[800,800]{1,0:T(8,128)(2,1)S(1)} %broadcast_select_fusion.6), channel_id=1, source_target_pairs={{0,56},{8,0},{16,8},{24,16},{32,24},{40,32},{48,40},{56,48},{1,57}... | collective-permute-start | bytes 3840008 | tf_op jit(solution)/shard_map/ppermute | solution.py:9
  181.9 33.6 %collective-permute-start.6 = (bf16[800,800]{1,0:T(8,128)(2,1)S(1)}, bf16[800,800]{1,0:T(8,128)(2,1)S(1)}, u32[]{:S(2)}, u32[]{:S(2)}) collective-permute-start(bf16[800,800]{1,0:T(8,128)(2,1)S(1)} %broadcast_select_fusion.12), channel_id=1, source_target_pairs={{0,7},{1,0},{2,1},{3,2},{4,3},{5,4},{6,5},{7,6},{8,15},{9,8},{10,9... | collective-permute-start | bytes 3840008 | tf_op jit(solution)/shard_map/ppermute | solution.py:9
  196.9 58.6 %copy-start.9 = (bf16[800,800]{1,0:T(8,128)(2,1)}, bf16[800,800]{1,0:T(8,128)(2,1)S(1)}, u32[]{:S(2)}) copy-start(bf16[800,800]{1,0:T(8,128)(2,1)S(1)} %collective-permute-done.7) | copy-start | bytes 3840004
  196.9 23.2 %collective-permute-start.9 = (bf16[800,800]{1,0:T(8,128)(2,1)S(1)}, bf16[800,800]{1,0:T(8,128)(2,1)S(1)}, u32[]{:S(2)}, u32[]{:S(2)}) collective-permute-start(bf16[800,800]{1,0:T(8,128)(2,1)S(1)} %collective-permute-done.7), channel_id=1, source_target_pairs={{0,56},{8,0},{16,8},{24,16},{32,24},{40,32},{48,40},{56,48},{1,57}... | collective-permute-start | bytes 3840008 | tf_op jit(solution)/shard_map/ppermute | solution.py:9
  215.5 33.6 %collective-permute-start.8 = (bf16[800,800]{1,0:T(8,128)(2,1)S(1)}, bf16[800,800]{1,0:T(8,128)(2,1)S(1)}, u32[]{:S(2)}, u32[]{:S(2)}) collective-permute-start(bf16[800,800]{1,0:T(8,128)(2,1)S(1)} %collective-permute-done.6), channel_id=1, source_target_pairs={{0,7},{1,0},{2,1},{3,2},{4,3},{5,4},{6,5},{7,6},{8,15},{9,8},{10,9... | collective-permute-start | bytes 3840008 | tf_op jit(solution)/shard_map/ppermute | solution.py:9
  220.1 37.2 %copy-start.11 = (bf16[800,800]{1,0:T(8,128)(2,1)}, bf16[800,800]{1,0:T(8,128)(2,1)S(1)}, u32[]{:S(2)}) copy-start(bf16[800,800]{1,0:T(8,128)(2,1)S(1)} %collective-permute-done.9) | copy-start | bytes 3840004
  220.1 39.0 %collective-permute-start.11 = (bf16[800,800]{1,0:T(8,128)(2,1)S(1)}, bf16[800,800]{1,0:T(8,128)(2,1)S(1)}, u32[]{:S(2)}, u32[]{:S(2)}) collective-permute-start(bf16[800,800]{1,0:T(8,128)(2,1)S(1)} %collective-permute-done.9), channel_id=1, source_target_pairs={{0,56},{8,0},{16,8},{24,16},{32,24},{40,32},{48,40},{56,48},{1,57}... | collective-permute-start | bytes 3840008 | tf_op jit(solution)/shard_map/ppermute | solution.py:9
  249.1 32.7 %collective-permute-start.10 = (bf16[800,800]{1,0:T(8,128)(2,1)S(1)}, bf16[800,800]{1,0:T(8,128)(2,1)S(1)}, u32[]{:S(2)}, u32[]{:S(2)}) collective-permute-start(bf16[800,800]{1,0:T(8,128)(2,1)S(1)} %collective-permute-done.8), channel_id=1, source_target_pairs={{0,7},{1,0},{2,1},{3,2},{4,3},{5,4},{6,5},{7,6},{8,15},{9,8},{10,9... | collective-permute-start | bytes 3840008 | tf_op jit(solution)/shard_map/ppermute | solution.py:9
  259.1 22.7 %copy-start.1 = (bf16[800,800]{1,0:T(8,128)(2,1)}, bf16[800,800]{1,0:T(8,128)(2,1)S(1)}, u32[]{:S(2)}) copy-start(bf16[800,800]{1,0:T(8,128)(2,1)S(1)} %collective-permute-done.11) | copy-start | bytes 3840004
  285.3 385.6 %all-reduce.5.cloned.1.call-start = ((), (), s32[]{:S(2)}) async-start(), calls=%async_computation.3 | async-start | bytes 5734400 | tf_op jit(solution)/shard_map/psum | solution.py:116
  383.0 33.6 %copy-start = (bf16[800,800]{1,0:T(8,128)(2,1)}, bf16[800,800]{1,0:T(8,128)(2,1)S(1)}, u32[]{:S(2)}) copy-start(bf16[800,800]{1,0:T(8,128)(2,1)S(1)} %multiply_convert_fusion.1) | copy-start | bytes 3840004
  383.0 33.4 %collective-permute-start.12 = (bf16[800,800]{1,0:T(8,128)(2,1)S(1)}, bf16[800,800]{1,0:T(8,128)(2,1)S(1)}, u32[]{:S(2)}, u32[]{:S(2)}) collective-permute-start(bf16[800,800]{1,0:T(8,128)(2,1)S(1)} %multiply_convert_fusion.1), channel_id=1, source_target_pairs={{0,7},{1,0},{2,1},{3,2},{4,3},{5,4},{6,5},{7,6},{8,15},{9,8},{10,9... | collective-permute-start | bytes 3840008 | tf_op jit(solution)/shard_map/ppermute | solution.py:9
  416.6 33.7 %collective-permute-start.13 = (bf16[800,800]{1,0:T(8,128)(2,1)S(1)}, bf16[800,800]{1,0:T(8,128)(2,1)S(1)}, u32[]{:S(2)}, u32[]{:S(2)}) collective-permute-start(bf16[800,800]{1,0:T(8,128)(2,1)S(1)} %broadcast_select_fusion.7), channel_id=1, source_target_pairs={{0,6},{1,7},{2,0},{3,1},{4,2},{5,3},{6,4},{7,5},{8,14},{9,15},{10,... | collective-permute-start | bytes 3840008 | tf_op jit(solution)/shard_map/ppermute | solution.py:9
  450.5 101.3 %copy-start.4 = (bf16[800,800]{1,0:T(8,128)(2,1)S(1)}, bf16[800,800]{1,0:T(8,128)(2,1)}, u32[]{:S(2)}) copy-start(bf16[800,800]{1,0:T(8,128)(2,1)} %copy-done.3) | copy-start | bytes 3840004
  450.5 31.4 %collective-permute-start.14 = (bf16[800,800]{1,0:T(8,128)(2,1)S(1)}, bf16[800,800]{1,0:T(8,128)(2,1)S(1)}, u32[]{:S(2)}, u32[]{:S(2)}) collective-permute-start(bf16[800,800]{1,0:T(8,128)(2,1)S(1)} %broadcast_select_fusion.9), channel_id=1, source_target_pairs={{0,4},{1,5},{2,6},{3,7},{4,0},{5,1},{6,2},{7,3},{8,12},{9,13},{10,... | collective-permute-start | bytes 3840008 | tf_op jit(solution)/shard_map/ppermute | solution.py:9
  482.1 71.6 %copy-start.10 = (bf16[800,800]{1,0:T(8,128)(2,1)S(1)}, bf16[800,800]{1,0:T(8,128)(2,1)}, u32[]{:S(2)}) copy-start(bf16[800,800]{1,0:T(8,128)(2,1)} %copy-done.9) | copy-start | bytes 3840004
  482.1 33.5 %collective-permute-start.15 = (bf16[800,800]{1,0:T(8,128)(2,1)S(1)}, bf16[800,800]{1,0:T(8,128)(2,1)S(1)}, u32[]{:S(2)}, u32[]{:S(2)}) collective-permute-start(bf16[800,800]{1,0:T(8,128)(2,1)S(1)} %broadcast_select_fusion.11), channel_id=1, source_target_pairs={{0,7},{1,0},{2,1},{3,2},{4,3},{5,4},{6,5},{7,6},{8,15},{9,8},{10,9... | collective-permute-start | bytes 3840008 | tf_op jit(solution)/shard_map/ppermute | solution.py:9
  515.6 31.7 %collective-permute-start.16 = (bf16[800,800]{1,0:T(8,128)(2,1)S(1)}, bf16[800,800]{1,0:T(8,128)(2,1)S(1)}, u32[]{:S(2)}, u32[]{:S(2)}) collective-permute-start(bf16[800,800]{1,0:T(8,128)(2,1)S(1)} %collective-permute-done.15), channel_id=1, source_target_pairs={{0,7},{1,0},{2,1},{3,2},{4,3},{5,4},{6,5},{7,6},{8,15},{9,8},{10,9... | collective-permute-start | bytes 3840008 | tf_op jit(solution)/shard_map/ppermute | solution.py:9
  547.2 30.8 %collective-permute-start.17 = (bf16[800,800]{1,0:T(8,128)(2,1)S(1)}, bf16[800,800]{1,0:T(8,128)(2,1)S(1)}, u32[]{:S(2)}, u32[]{:S(2)}) collective-permute-start(bf16[800,800]{1,0:T(8,128)(2,1)S(1)} %collective-permute-done.16), channel_id=1, source_target_pairs={{0,7},{1,0},{2,1},{3,2},{4,3},{5,4},{6,5},{7,6},{8,15},{9,8},{10,9... | collective-permute-start | bytes 3840008 | tf_op jit(solution)/shard_map/ppermute | solution.py:9
  553.6 1.8 copy-start.12
  555.4 22.6 %copy-start.2 = (bf16[800,800]{1,0:T(8,128)(2,1)S(1)}, bf16[800,800]{1,0:T(8,128)(2,1)}, u32[]{:S(2)}) copy-start(bf16[800,800]{1,0:T(8,128)(2,1)} %copy-done.1) | copy-start | bytes 3840004
  683.4 32.6 %all-to-all-start.1 = ((bf16[64,100,100]{2,1,0:T(8,128)(2,1)}), bf16[64,100,100]{2,1,0:T(8,128)(2,1)S(1)}, u32[]{:S(2)}, u32[]{:S(2)}) async-start(bf16[64,100,100]{2,1,0:T(8,128)(2,1)} %copy.44), calls=%async_computation.1 | async-start | bytes 3407872 | tf_op jit(solution)/shard_map/all_to_all | solution.py:121
  (3 other events, 2.5 us)
Sparse Core Ops, SparseCore 0:
  285.4 94.5 all-reduce.2
  581.7 89.1 all-reduce.4
where the time goes:
time: 740 us; the launch traced here: 730 us
  waiting for transfers between devices  566 us (76%)
  starting transfers between devices  74.1 us (10%)
  local copies, waits for them, and re-layouts  37.1 us (5%)
  other arithmetic  20.8 us (3%)
  matrix products  17.7 us (2%)
  between operations  14.4 us (2%)
    ppermute x18, waiting for transfers between devices, passed_along(): lax.ppermute(array, axis, [(i, (i + by) % count) for i in range(count)])  341 us
    psum x1, waiting for transfers between devices, per_device(): square_full = lax.psum(square_part, 'layer')  91.6 us
    psum x1, waiting for transfers between devices, per_device(): cube = lax.psum(cube_part, 'layer')  84 us
    ppermute x18, starting transfers between devices, passed_along(): lax.ppermute(array, axis, [(i, (i + by) % count) for i in range(count)])  56.8 us
    all_to_all x1, waiting for transfers between devices, per_device(): lax.all_to_all(outgoing, ('row', 'col'), split_axis=0, concat_axis=0, til...  24.4 us
    all_to_all x1, waiting for transfers between devices, per_device(): lax.all_to_all(pieces, ('row', 'col'), split_axis=0, concat_axis=0, tiled...  24.3 us
  transfers between devices with their start and end apart: 22, of which 19 were waited for; matrix products, arithmetic and copies ran while one was open for 3% of the time, Pallas kernels for 0%

commit v1 on v0

v1 whole, which is shorter than its diff:
```python
import jax
import jax.numpy as jnp
from jax import lax
from jax.sharding import PartitionSpec as P


def apply_pattern(values, pattern):
    count = pattern.shape[0]
    rows = values.shape[0] // count
    cols = values.shape[1] // count
    shaped = values.reshape(count, rows, count, cols)
    shaped = shaped * pattern[:, None, :, None].astype(values.dtype)
    return shaped.reshape(count * rows, count * cols)


def group_order(mapping, group, tile_blocks):
    return jnp.argsort(lax.dynamic_slice_in_dim(mapping, group * tile_blocks, tile_blocks))


def source_groups(mapping, group, tile_blocks):
    return lax.dynamic_slice_in_dim(mapping, group * tile_blocks, tile_blocks) // tile_blocks


def per_device(density, density_mask, square_mask, result_mask, block_perm):
    groups = lax.axis_size("row")
    tile_blocks = density_mask.shape[0]
    width = density.shape[0] // tile_blocks
    half = width // lax.axis_size("layer")
    row_id = lax.axis_index("row")
    col_id = lax.axis_index("col")
    layer_id = lax.axis_index("layer")
    inverse = jnp.argsort(block_perm).astype(jnp.int32)

    masked = apply_pattern(density, density_mask)
    shaped = masked.reshape(tile_blocks, width, tile_blocks, width)
    shaped = jnp.take(shaped, group_order(block_perm, row_id, tile_blocks), axis=0)
    shaped = jnp.take(shaped, group_order(block_perm, col_id, tile_blocks), axis=2)
    pieces = shaped.transpose(0, 2, 1, 3).reshape(groups * groups, width, width)
    received = lax.all_to_all(pieces, ("row", "col"), split_axis=0, concat_axis=0, tiled=True)
    shaped = received.reshape(groups, groups, width, width).transpose(0, 2, 1, 3)
    shaped = jnp.take(shaped, source_groups(inverse, row_id, tile_blocks), axis=0)
    shaped = jnp.take(shaped, source_groups(inverse, col_id, tile_blocks), axis=2)
    grid_tile = shaped.reshape(tile_blocks * width, tile_blocks * width)

    grid_half = lax.dynamic_index_in_dim(
        grid_tile.reshape(tile_blocks, 2, half, tile_blocks * width), layer_id, axis=1, keepdims=False
    ).reshape(tile_blocks * half, tile_blocks * width)
    left = lax.all_gather(grid_half, "col", axis=1, tiled=True)
    right = lax.all_gather(grid_tile, "row", axis=0, tiled=True)

    square_acc = jnp.dot(left, right, preferred_element_type=jnp.float32)
    square = apply_pattern(square_acc, square_mask).astype(jnp.bfloat16)

    square_left = lax.all_gather(square, "col", axis=1, tiled=True)
    cube = jnp.dot(square_left, right, preferred_element_type=jnp.float32)
    result = apply_pattern(3.0 * square.astype(jnp.float32) - 2.0 * cube, result_mask).astype(jnp.bfloat16)

    shaped = result.reshape(tile_blocks, half, tile_blocks, width)
    shaped = jnp.take(shaped, group_order(inverse, row_id, tile_blocks), axis=0)
    shaped = jnp.take(shaped, group_order(inverse, col_id, tile_blocks), axis=2)
    pieces = shaped.transpose(0, 2, 1, 3).reshape(groups * groups, half, width)
    pieces = jnp.concatenate([pieces, pieces], axis=0)
    returned = lax.all_to_all(pieces, ("layer", "row", "col"), split_axis=0, concat_axis=0, tiled=True)
    shaped = returned.reshape(2, groups, groups, half, width).transpose(1, 0, 3, 2, 4)
    shaped = shaped.reshape(groups, width, groups, width)
    shaped = jnp.take(shaped, source_groups(block_perm, row_id, tile_blocks), axis=0)
    shaped = jnp.take(shaped, source_groups(block_perm, col_id, tile_blocks), axis=2)
    return shaped.reshape(tile_blocks * width, tile_blocks * width)


def solution(mesh):
    in_specs = (P("row", "col"), P("row", "col"), P("row", "col"), P("row", "col"), P())
    out_specs = P("row", "col")
    return jax.shard_map(
        per_device, mesh=mesh, in_specs=in_specs, out_specs=out_specs, check_vma=False
    )
```

time: 740 us -> 358 us (0.48); the launches traced: 730 us -> 357 us
  waiting for transfers between devices: 566 us -> 225 us
  starting transfers between devices: 74.1 us -> 17.1 us
  local copies, waits for them, and re-layouts: 37.1 us -> 68.6 us
  other arithmetic: 20.8 us -> 9.74 us
    ppermute x18 -> x0, waiting for transfers between devices: 341 us -> none  [passed_along(): lax.ppermute(array, axis, [(i, (i + by) % count) for i in range(count)])]
    psum x2 -> x0, waiting for transfers between devices: 176 us -> none  [the longest x1 91.6 us: per_device(): square_full = lax.psum(square_part, 'layer')]
    all_gather x0 -> x3, waiting for transfers between devices: none -> 173 us  [the longest x1 64.8 us: per_device(): square_left = lax.all_gather(square, 'col', axis=1, tiled=True)]
    ppermute x18 -> x0, starting transfers between devices: 56.8 us -> none  [passed_along(): lax.ppermute(array, axis, [(i, (i + by) % count) for i in range(count)])]
    unnamed x26 -> x10, local copies, waits for them, and re-layouts: 2.41 us -> 20.5 us
    all_gather x0 -> x2, local copies, waits for them, and re-layouts: none -> 12.5 us  [the longest x1 6.27 us: per_device(): left = lax.all_gather(grid_half, 'col', axis=1, tiled=True)]
    dot_general x8 -> x2, matrix products: 17.7 us -> 22.9 us  [the longest x1 11.5 us: per_device(): cube = jnp.dot(square_left, right, preferred_element_type=jnp.float32)]
  transfers between devices with their start and end apart: 22 -> 5, of which waited for: 19 -> 5; matrix products, arithmetic and copies ran while one was open for 3% -> 6% of each run, Pallas kernels for 0% -> 0%
where the time goes in v1:
time: 358 us; the launch traced here: 357 us
  waiting for transfers between devices  225 us (63%)
  local copies, waits for them, and re-layouts  68.6 us (19%)
  matrix products  22.9 us (6%)
  starting transfers between devices  17.1 us (5%)
  between operations  13.5 us (4%)
  other arithmetic  9.74 us (3%)
    all_gather x1, waiting for transfers between devices, per_device(): square_left = lax.all_gather(square, 'col', axis=1, tiled=True)  64.8 us
    all_gather x1, waiting for transfers between devices, per_device(): left = lax.all_gather(grid_half, 'col', axis=1, tiled=True)  62 us
    all_gather x1, waiting for transfers between devices, per_device(): right = lax.all_gather(grid_tile, 'row', axis=0, tiled=True)  46.4 us
    all_to_all x1, waiting for transfers between devices, per_device(): lax.all_to_all(pieces, ('layer', 'row', 'col'), split_axis=0, concat_axis...  27.2 us
    all_to_all x1, waiting for transfers between devices, per_device(): lax.all_to_all(pieces, ('row', 'col'), split_axis=0, concat_axis=0, tiled...  24.5 us
    unnamed x10, local copies, waits for them, and re-layouts  20.5 us
    dot_general x1, matrix products, per_device(): cube = jnp.dot(square_left, right, preferred_element_type=jnp.float32)  11.5 us
    dot_general x1, matrix products, per_device(): square_acc = jnp.dot(left, right, preferred_element_type=jnp.float32)  11.5 us
  transfers between devices with their start and end apart: 5, of which 5 were waited for; matrix products, arithmetic and copies ran while one was open for 6% of the time, Pallas kernels for 0%

profile of v1, /device:TPU:0, one launch (start us, length us, event | category | flops | bytes accessed | tf_op | source)
XLA Modules:
  0.0 356.8 jit_solution(5024438377983922619)
XLA Ops:
  6.5 2.7 sort.76
  12.0 3.4 reshape.63
  16.8 1.1 copy.45
  17.9 1.2 gather_fusion.3
  19.3 1.1 copy.70
  20.3 2.3 copy.47
  22.6 9.4 %all-to-all-start = ((bf16[64,100,100]{2,1,0:T(8,128)(2,1)}), bf16[64,100,100]{2,1,0:T(8,128)(2,1)S(1)}, u32[]{:S(2)}, u32[]{:S(2)}) async-start(bf16[64,100,100]{2,1,0:T(8,128)(2,1)} %copy.47), calls=%async_computation | async-start | bytes 3407872 | tf_op jit(solution)/shard_map/all_to_all | solution.py:39
  32.3 24.5 %all-to-all-done = bf16[64,100,100]{2,1,0:T(8,128)(2,1)S(1)} async-done(((bf16[64,100,100]{2,1,0:T(8,128)(2,1)}), bf16[64,100,100]{2,1,0:T(8,128)(2,1)S(1)}, u32[]{:S(2)}, u32[]{:S(2)}) %all-to-all-start) | async-done | bytes 1280032 | tf_op jit(solution)/shard_map/all_to_all | solution.py:39
  58.1 1.1 copy.50
  59.1 1.2 gather_fusion.5
  60.6 1.1 copy.51
  61.6 2.1 reshape_reshape.3
  63.8 1.2 constant_dynamic-slice_fusion
  65.0 1.2 reshape.66
  66.9 2.2 reshape.67
  69.9 62.0 %all-gather.8.cloned.1.call-done = bf16[8,800,400]{1,2,0:T(8,128)(2,1)} async-done(((bf16[1,800,400]{1,2,0:T(8,128)(2,1)}), bf16[8,800,400]{1,2,0:T(8,128)(2,1)}) %all-gather.8.cloned.1.call-update) | async-done | bytes 5120016 | tf_op jit(solution)/shard_map/all_gather | solution.py:48
  131.9 6.3 %copy.53 = bf16[8,800,400]{1,0,2:T(8,128)(2,1)} copy(bf16[8,800,400]{1,2,0:T(8,128)(2,1)} %all-gather.8.cloned.1.call-done) | data formatting | bytes 10240000 | tf_op jit(solution)/shard_map/all_gather | solution.py:48
  138.2 10.4 %reshape.146 = bf16[6400,400]{0,1:T(8,128)(2,1)} reshape(bf16[8,800,400]{1,0,2:T(8,128)(2,1)} %copy.53) | data formatting | bytes 10240000
  148.6 46.4 %all-gather.6.cloned.1.call-done = bf16[6400,800]{1,0:T(8,128)(2,1)} async-done(((bf16[800,800]{1,0:T(8,128)(2,1)}), bf16[6400,800]{1,0:T(8,128)(2,1)}) %all-gather.6.cloned.1.call-update) | async-done | bytes 10240016 | tf_op jit(solution)/shard_map/all_gather | solution.py:49
  195.0 11.5 %fusion = bf16[400,800]{1,0:T(8,128)(2,1)} fusion(f32[400,800]{1,0:T(8,128)S(1)} %mul.59, bf16[6400,400]{0,1:T(8,128)(2,1)} %reshape.146, bf16[6400,800]{1,0:T(8,128)(2,1)} %all-gather.6.cloned.1.call-done), kind=kOutput, calls=%fused_computation.20 | convolution fusion | flops 4096640000 | bytes 17280000 | tf_op jit(solution)/shard_map/dot_general | solution.py:51
  208.2 1.0 sort.77
  209.2 64.8 %all-gather.10.cloned.1.call-done = bf16[8,800,400]{1,2,0:T(8,128)(2,1)} async-done(((bf16[1,800,400]{1,2,0:T(8,128)(2,1)}), bf16[8,800,400]{1,2,0:T(8,128)(2,1)}) %all-gather.10.cloned.1.call-update) | async-done | bytes 5120016 | tf_op jit(solution)/shard_map/all_gather | solution.py:54
  274.0 6.3 %copy.55 = bf16[8,800,400]{1,0,2:T(8,128)(2,1)} copy(bf16[8,800,400]{1,2,0:T(8,128)(2,1)} %all-gather.10.cloned.1.call-done) | data formatting | bytes 10240000 | tf_op jit(solution)/shard_map/all_gather | solution.py:54
  280.3 10.1 %reshape.148 = bf16[6400,400]{0,1:T(8,128)(2,1)} reshape(bf16[8,800,400]{1,0,2:T(8,128)(2,1)} %copy.55) | data formatting | bytes 10240000
  290.4 11.5 %multiply_convert_fusion = bf16[400,800]{1,0:T(8,128)(2,1)} fusion(f32[400,800]{1,0:T(8,128)S(1)} %mul.66, bf16[400,800]{1,0:T(8,128)(2,1)S(1)} %copy-done, bf16[6400,400]{0,1:T(8,128)(2,1)} %reshape.148, bf16[6400,800]{1,0:T(8,128)(2,1)} %all-gather.6.cloned.1.call-done), kind=kOutput, calls=%fused_computation.19 | convolution fusion | flops 4097920000 | bytes 17920000 | tf_op jit(solution)/shard_map/dot_general | solution.py:55
  301.9 2.1 reshape.68
  306.8 2.3 copy.58
  309.1 7.4 %all-to-all-start.1 = ((bf16[128,50,100]{2,1,0:T(8,128)(2,1)}), bf16[128,50,100]{2,1,0:T(8,128)(2,1)S(1)}, u32[]{:S(2)}, u32[]{:S(2)}) async-start(bf16[128,50,100]{2,1,0:T(8,128)(2,1)} %copy.58), calls=%async_computation.1 | async-start | bytes 3670016 | tf_op jit(solution)/shard_map/all_to_all | solution.py:63
  316.5 27.2 %all-to-all-done.1 = bf16[128,50,100]{2,1,0:T(8,128)(2,1)S(1)} async-done(((bf16[128,50,100]{2,1,0:T(8,128)(2,1)}), bf16[128,50,100]{2,1,0:T(8,128)(2,1)S(1)}, u32[]{:S(2)}, u32[]{:S(2)}) %all-to-all-start.1) | async-done | bytes 1280032 | tf_op jit(solution)/shard_map/all_to_all | solution.py:63
  345.0 1.1 copy.61
  346.1 1.2 gather_fusion.7
  348.1 2.1 reshape.72
  (68 shorter events, 14.2 us)
Async XLA Ops:
  6.5 8.9 %copy-start.1 = (s32[8,8]{1,0:T(8,128)S(1)}, s32[8,8]{1,0:T(8,128)}, u32[]{:S(2)}) copy-start(s32[8,8]{1,0:T(8,128)} %param.10) | copy-start | bytes 772
  22.6 34.2 %all-to-all-start = ((bf16[64,100,100]{2,1,0:T(8,128)(2,1)}), bf16[64,100,100]{2,1,0:T(8,128)(2,1)S(1)}, u32[]{:S(2)}, u32[]{:S(2)}) async-start(bf16[64,100,100]{2,1,0:T(8,128)(2,1)} %copy.47), calls=%async_computation | async-start | bytes 3407872 | tf_op jit(solution)/shard_map/all_to_all | solution.py:39
  32.0 99.9 %all-gather.8.cloned.1.call-start = ((), (), s32[]{:S(2)}) async-start(), calls=%async_computation.3 | async-start | bytes 6451200 | tf_op jit(solution)/shard_map/all_gather | solution.py:48
  66.2 128.7 %all-gather.6.cloned.1.call-start = ((), (), s32[]{:S(2)}) async-start(), calls=%async_computation.2 | async-start | bytes 12902400 | tf_op jit(solution)/shard_map/all_gather | solution.py:49
  66.9 2.2 copy-start.2
  69.1 204.9 %all-gather.10.cloned.1.call-start = ((), (), s32[]{:S(2)}) async-start(), calls=%async_computation.4 | async-start | bytes 6451200 | tf_op jit(solution)/shard_map/all_gather | solution.py:54
  148.6 57.9 %copy-start.3 = (s32[8,8]{1,0:T(8,128)S(1)}, s32[8,8]{1,0:T(8,128)}, u32[]{:S(2)}) copy-start(s32[8,8]{1,0:T(8,128)} %param.12) | copy-start | bytes 772
  280.3 10.1 %copy-start = (bf16[400,800]{1,0:T(8,128)(2,1)S(1)}, bf16[400,800]{1,0:T(8,128)(2,1)}, u32[]{:S(2)}) copy-start(bf16[400,800]{1,0:T(8,128)(2,1)} %fusion) | copy-start | bytes 1920004
  309.1 34.6 %all-to-all-start.1 = ((bf16[128,50,100]{2,1,0:T(8,128)(2,1)}), bf16[128,50,100]{2,1,0:T(8,128)(2,1)S(1)}, u32[]{:S(2)}, u32[]{:S(2)}) async-start(bf16[128,50,100]{2,1,0:T(8,128)(2,1)} %copy.58), calls=%async_computation.1 | async-start | bytes 3670016 | tf_op jit(solution)/shard_map/all_to_all | solution.py:63
Sparse Core Ops, SparseCore 0:
  66.4 65.5 all-gather.7
  133.6 61.3 all-gather.5
  206.6 67.3 all-gather.9

commit v2 on v1

--- a/solution.py
+++ b/solution.py
@@ -45,14 +45,14 @@
     grid_half = lax.dynamic_index_in_dim(
         grid_tile.reshape(tile_blocks, 2, half, tile_blocks * width), layer_id, axis=1, keepdims=False
     ).reshape(tile_blocks * half, tile_blocks * width)
-    left = lax.all_gather(grid_half, "col", axis=1, tiled=True)
-    right = lax.all_gather(grid_tile, "row", axis=0, tiled=True)
+    left = lax.all_gather(grid_half, "col", axis=0, tiled=False)
+    right = lax.all_gather(grid_tile, "row", axis=0, tiled=False)
 
-    square_acc = jnp.dot(left, right, preferred_element_type=jnp.float32)
+    square_acc = jnp.einsum("gik,gkj->ij", left, right, preferred_element_type=jnp.float32)
     square = apply_pattern(square_acc, square_mask).astype(jnp.bfloat16)
 
-    square_left = lax.all_gather(square, "col", axis=1, tiled=True)
-    cube = jnp.dot(square_left, right, preferred_element_type=jnp.float32)
+    square_left = lax.all_gather(square, "col", axis=0, tiled=False)
+    cube = jnp.einsum("gik,gkj->ij", square_left, right, preferred_element_type=jnp.float32)
     result = apply_pattern(3.0 * square.astype(jnp.float32) - 2.0 * cube, result_mask).astype(jnp.bfloat16)
 
     shaped = result.reshape(tile_blocks, half, tile_blocks, width)

time: 358 us -> 341 us (0.953)
  local copies, waits for them, and re-layouts: 68.6 us -> 34.6 us
  waiting for transfers between devices: 225 us -> 241 us
    unnamed x10 -> x4, local copies, waits for them, and re-layouts: 20.5 us -> 0.01 us
    all_gather x3, waiting for transfers between devices: 173 us -> 190 us  [the longest x1 64.8 us: per_device(): square_left = lax.all_gather(square, 'col', axis=0, tiled=False)]
    all_gather x2 -> x0, local copies, waits for them, and re-layouts: 12.5 us -> none  [the longest x1 6.27 us: per_device(): left = lax.all_gather(grid_half, 'col', axis=1, tiled=True)]
  transfers between devices with their start and end apart: 5 -> 5, of which waited for: 5 -> 5; matrix products, arithmetic and copies ran while one was open for 6% -> 2% of each run, Pallas kernels for 0% -> 0%
where the time goes in v2:
time: 341 us
  waiting for transfers between devices  241 us (71%)
  local copies, waits for them, and re-layouts  34.6 us (10%)
  matrix products  23.7 us (7%)
  starting transfers between devices  17.3 us (5%)
  between operations  13.5 us (4%)
  other arithmetic  10.4 us (3%)
    all_gather x1, waiting for transfers between devices, per_device(): square_left = lax.all_gather(square, 'col', axis=0, tiled=False)  64.8 us
    all_gather x1, waiting for transfers between devices, per_device(): right = lax.all_gather(grid_tile, 'row', axis=0, tiled=False)  63.1 us
    all_gather x1, waiting for transfers between devices, per_device(): left = lax.all_gather(grid_half, 'col', axis=0, tiled=False)  61.8 us
    all_to_all x1, waiting for transfers between devices, per_device(): lax.all_to_all(pieces, ('layer', 'row', 'col'), split_axis=0, concat_axis...  27.2 us
    all_to_all x1, waiting for transfers between devices, per_device(): lax.all_to_all(pieces, ('row', 'col'), split_axis=0, concat_axis=0, tiled...  24.5 us
    dot_general x1, matrix products, per_device(): jnp.einsum('gik,gkj->ij', left, right, preferred_element_type=jnp.float32)  12.2 us
    dot_general x1, matrix products, per_device(): jnp.einsum('gik,gkj->ij', square_left, right, preferred_element_type=jnp....  11.4 us
    all_to_all x1, starting transfers between devices, per_device(): lax.all_to_all(pieces, ('row', 'col'), split_axis=0, concat_axis=0, tiled...  9.41 us
  transfers between devices with their start and end apart: 5, of which 5 were waited for; matrix products, arithmetic and copies ran while one was open for 2% of the time, Pallas kernels for 0%

profile of v2, /device:TPU:0, one launch (start us, length us, event | category | flops | bytes accessed | tf_op | source)
XLA Modules:
  0.0 340.9 jit_solution(7390733582008280915)
XLA Ops:
  6.5 2.7 sort.76
  10.1 1.0 sort.80
  11.0 1.0 sort.79
  12.7 3.4 %reshape.57 = bf16[8,100,8,100]{3,2,1,0:T(8,128)(2,1)S(1)} reshape(bf16[800,800]{1,0:T(8,128)(2,1)} %param.9) | data formatting | bytes 2560000 | tf_op jit(solution)/shard_map/reshape | solution.py:11
  16.3 0.9 gather_fusion.2
  17.4 1.1 copy.39
  18.5 1.2 gather_fusion.3
  19.9 1.1 copy.62
  21.0 2.3 copy.41
  23.2 9.4 %all-to-all-start = ((bf16[64,100,100]{2,1,0:T(8,128)(2,1)}), bf16[64,100,100]{2,1,0:T(8,128)(2,1)S(1)}, u32[]{:S(2)}, u32[]{:S(2)}) async-start(bf16[64,100,100]{2,1,0:T(8,128)(2,1)} %copy.41), calls=%async_computation | async-start | bytes 3407872 | tf_op jit(solution)/shard_map/all_to_all | solution.py:39
  32.9 24.5 %all-to-all-done = bf16[64,100,100]{2,1,0:T(8,128)(2,1)S(1)} async-done(((bf16[64,100,100]{2,1,0:T(8,128)(2,1)}), bf16[64,100,100]{2,1,0:T(8,128)(2,1)S(1)}, u32[]{:S(2)}, u32[]{:S(2)}) %all-to-all-start) | async-done | bytes 1280032 | tf_op jit(solution)/shard_map/all_to_all | solution.py:39
  58.7 1.1 copy.44
  59.8 1.2 gather_fusion.5
  61.2 1.1 copy.45
  62.3 2.1 reshape_reshape.3
  64.4 1.2 constant_dynamic-slice_fusion
  65.7 1.2 all_gather_reshape.6
  67.6 2.2 all_gather_reshape.7
  70.8 61.8 %all-gather.5.cloned.1.call-done = bf16[8,400,800]{2,1,0:T(8,128)(2,1)} async-done(((bf16[1,400,800]{2,1,0:T(8,128)(2,1)}), bf16[8,400,800]{2,1,0:T(8,128)(2,1)}) %all-gather.5.cloned.1.call-update) | async-done | bytes 5120016 | tf_op jit(solution)/shard_map/all_gather | solution.py:48
  132.6 63.1 %all-gather.7.cloned.1.call-done = bf16[8,800,800]{2,1,0:T(8,128)(2,1)} async-done(((bf16[1,800,800]{2,1,0:T(8,128)(2,1)}), bf16[8,800,800]{2,1,0:T(8,128)(2,1)}) %all-gather.7.cloned.1.call-update) | async-done | bytes 10240016 | tf_op jit(solution)/shard_map/all_gather | solution.py:49
  195.6 12.2 %fusion.2 = bf16[400,800]{1,0:T(8,128)(2,1)} fusion(f32[400,800]{1,0:T(8,128)S(1)} %mul.59, bf16[8,400,800]{2,1,0:T(8,128)(2,1)} %all-gather.5.cloned.1.call-done, bf16[8,800,800]{2,1,0:T(8,128)(2,1)} %all-gather.7.cloned.1.call-done), kind=kOutput, calls=%fused_computation.22 | convolution fusion | flops 4096640000 | bytes 17280000 | tf_op jit(solution)/shard_map/gik,gkj->ij/dot_general | solution.py:51
  208.6 1.0 sort.78
  209.6 1.0 sort.77
  210.6 64.8 %all-gather.9.cloned.1.call-done = bf16[3200,800]{1,0:T(8,128)(2,1)} async-done(((bf16[400,800]{1,0:T(8,128)(2,1)}), bf16[3200,800]{1,0:T(8,128)(2,1)}) %all-gather.9.cloned.1.call-update) | async-done | bytes 5120016 | tf_op jit(solution)/shard_map/all_gather | solution.py:54
  275.4 11.4 %multiply_convert_fusion = bf16[400,800]{1,0:T(8,128)(2,1)S(1)} fusion(f32[400,800]{1,0:T(8,128)S(1)} %mul.66, bf16[400,800]{1,0:T(8,128)(2,1)} %fusion.2, bf16[8,400,800]{2,1,0:T(8,128)(2,1)} %bitcast.61, bf16[8,800,800]{2,1,0:T(8,128)(2,1)} %all-gather.7.cloned.1.call-done), kind=kOutput, calls=%fused_computation.21 | convolution fusion | flops 4097920000 | bytes 17920000 | tf_op jit(solution)/shard_map/gik,gkj->ij/dot_general | solution.py:55
  286.9 1.0 reshape.60
  290.6 2.6 copy.50
  293.2 7.4 %all-to-all-start.1 = ((bf16[128,50,100]{2,1,0:T(8,128)(2,1)}), bf16[128,50,100]{2,1,0:T(8,128)(2,1)S(1)}, u32[]{:S(2)}, u32[]{:S(2)}) async-start(bf16[128,50,100]{2,1,0:T(8,128)(2,1)} %copy.50), calls=%async_computation.1 | async-start | bytes 3670016 | tf_op jit(solution)/shard_map/all_to_all | solution.py:63
  300.6 27.2 %all-to-all-done.1 = bf16[128,50,100]{2,1,0:T(8,128)(2,1)S(1)} async-done(((bf16[128,50,100]{2,1,0:T(8,128)(2,1)}), bf16[128,50,100]{2,1,0:T(8,128)(2,1)S(1)}, u32[]{:S(2)}, u32[]{:S(2)}) %all-to-all-start.1) | async-done | bytes 1280032 | tf_op jit(solution)/shard_map/all_to_all | solution.py:63
  329.1 1.1 copy.53
  330.2 1.2 gather_fusion.7
  332.2 2.1 reshape.64
  (60 shorter events, 11.4 us)
Async XLA Ops:
  23.2 34.2 %all-to-all-start = ((bf16[64,100,100]{2,1,0:T(8,128)(2,1)}), bf16[64,100,100]{2,1,0:T(8,128)(2,1)S(1)}, u32[]{:S(2)}, u32[]{:S(2)}) async-start(bf16[64,100,100]{2,1,0:T(8,128)(2,1)} %copy.41), calls=%async_computation | async-start | bytes 3407872 | tf_op jit(solution)/shard_map/all_to_all | solution.py:39
  32.6 99.9 %all-gather.5.cloned.1.call-start = ((), (), s32[]{:S(2)}) async-start(), calls=%async_computation.2 | async-start | bytes 6451200 | tf_op jit(solution)/shard_map/all_gather | solution.py:48
  66.9 128.7 %all-gather.7.cloned.1.call-start = ((), (), s32[]{:S(2)}) async-start(), calls=%async_computation.3 | async-start | bytes 12902400 | tf_op jit(solution)/shard_map/all_gather | solution.py:49
  67.6 2.5 copy-start
  69.8 205.6 %all-gather.9.cloned.1.call-start = ((), (), s32[]{:S(2)}) async-start(), calls=%async_computation.4 | async-start | bytes 6451200 | tf_op jit(solution)/shard_map/all_gather | solution.py:54
  70.8 137.1 %copy-start.1 = (s32[8,8]{1,0:T(8,128)S(1)}, s32[8,8]{1,0:T(8,128)}, u32[]{:S(2)}) copy-start(s32[8,8]{1,0:T(8,128)} %param.12) | copy-start | bytes 772
  293.2 34.6 %all-to-all-start.1 = ((bf16[128,50,100]{2,1,0:T(8,128)(2,1)}), bf16[128,50,100]{2,1,0:T(8,128)(2,1)S(1)}, u32[]{:S(2)}, u32[]{:S(2)}) async-start(bf16[128,50,100]{2,1,0:T(8,128)(2,1)} %copy.50), calls=%async_computation.1 | async-start | bytes 3670016 | tf_op jit(solution)/shard_map/all_to_all | solution.py:63
Sparse Core Ops, SparseCore 0:
  67.0 65.5 all-gather.4
  134.3 61.3 all-gather.6
  208.0 67.3 all-gather.8
